TPU v7x, 32 devices: a whole 2x2x4 slice. The times are simulated.
32 devices in a mesh: row: 4 (over z), col: 8 (over y, x, core).
Axes of the slice: x: 2, y: 2, z: 4, core: 2. Of those that a mesh axis runs over, the one named last changes fastest.
Arguments:
- image: float32 [224, 32, 2048], P(None, 'row', 'col'), may hold values from -24 to 24
- start_basis: float32 [224, 16], replicated, may hold values from -4 to 4
Outputs:
- smoothed: float32 [224, 32, 2048], P(None, 'row', 'col')
- lowrank: float32 [224, 32, 2048], P(None, 'row', 'col')
All inputs are finite; a program needn't handle non-finite values.
Results may differ from a plain program's by a relative error of at most 0.0003.
Values sent between devices are 32-bit elements; how exact they have to be, the bound alone decides.
No kernel may reach another device: no remote copies, remote signals or barrier semaphores. Data moves between devices by JAX's collectives and lax.ppermute only.
A program may use at most 64 MiB of HBM per device.

v0:
```python
import jax
import jax.numpy as jnp
from jax import lax
from jax.sharding import PartitionSpec as P

SWEEPS = 4
SUBIT = 2
tau_step = 0.22
fidelity = 0.1


def padded_2(cells, sides, width):
    for axis, dim in sides:
        count = lax.axis_size(axis)
        ends = count - 1
        head = lax.slice_in_dim(cells, 0, width, axis=dim)
        tail = lax.slice_in_dim(cells, cells.shape[dim] - width, cells.shape[dim], axis=dim)
        cells = jnp.concatenate(
            [
                lax.ppermute(tail, axis, [(i, (i + 1) % count) for i in range(ends)]),
                cells,
                lax.ppermute(head, axis, [((i + 1) % count, i) for i in range(ends)]),
            ],
            axis=dim,
        )
    return cells


def forward_diffs(padded):
    diff_col = padded[..., :-1, 1:] - padded[..., :-1, :-1]
    diff_row = padded[..., 1:, :-1] - padded[..., :-1, :-1]
    return (diff_col, diff_row)


def smooth_step(padded, source):
    diff_col, diff_row = forward_diffs(padded)
    energy_sum = jnp.sum(diff_col * diff_col + diff_row * diff_row, axis=0)
    weight = 1.0 / jnp.sqrt(1.0 + energy_sum / padded.shape[0])
    flux_col = weight * diff_col
    flux_row = weight * diff_row
    spread = (
        flux_col[..., 1:, 1:]
        - flux_col[..., 1:, :-1]
        + flux_row[..., 1:, 1:]
        - flux_row[..., :-1, 1:]
    )
    centre = padded[..., 1:-1, 1:-1]
    return centre + tau_step * spread + tau_step * fidelity * (source - centre)


def orthonormal(block):
    inner = jnp.dot(block.T, block, precision=lax.Precision.HIGHEST)
    lower = jnp.linalg.cholesky(inner)
    return lax.linalg.triangular_solve(lower, block, left_side=False, lower=True, transpose_a=True)


def shards(image, start_basis):
    band_count, tile_rows, tile_cols = image.shape
    field = image
    for sweep_no in range(SWEEPS):
        extended = padded_2(field, (("row", 1), ("col", 2)), 1)
        field = smooth_step(extended, image)
    flat_field = field.reshape(band_count, tile_rows * tile_cols)
    basis_now = start_basis
    local_gram = lax.dot_general(
        flat_field,
        flat_field,
        (((1,), (1,)), ((), ())),
        precision=lax.Precision.HIGHEST,
        preferred_element_type=jnp.float32,
    )
    gram_full = lax.psum(local_gram, ("row", "col"))
    for turn in range(SUBIT):
        product = jnp.dot(gram_full, basis_now, precision=lax.Precision.HIGHEST)
        basis_now = orthonormal(orthonormal(product))
    coeffs = jnp.dot(basis_now.T, flat_field, precision=lax.Precision.HIGHEST)
    lowrank = jnp.dot(basis_now, coeffs, precision=lax.Precision.HIGHEST)
    return (field, lowrank.reshape(band_count, tile_rows, tile_cols))


def solution(mesh):
    in_specs = (P(None, "row", "col"), P())
    out_specs = (P(None, "row", "col"), P(None, "row", "col"))
    return jax.shard_map(shards, mesh=mesh, in_specs=in_specs, out_specs=out_specs, check_vma=False)
```

profile of v0, /device:TPU:1, one launch (start us, length us, event | category | flops | bytes accessed | tf_op | source)
XLA Modules:
  0.0 325.3 jit_solution(15934660971049037170)
XLA Ops:
  7.2 2.4 fusion.42
  9.6 1.3 collective-permute-start.1
  10.9 4.7 %collective-permute-start = (f32[224,1,256]{2,0,1:T(8,128)S(1)}, f32[224,1,256]{2,0,1:T(8,128)S(1)}, u32[]{:S(2)}, u32[]{:S(2)}) collective-permute-start(f32[224,1,256]{2,0,1:T(8,128)S(1)} %copy.216), channel_id=1, source_target_pairs={{0,8},{8,16},{16,24},{1,9},{9,17},{17,25},{2,10},{10,18},{18,26},{... | collective-permute-start | bytes 688136 | tf_op jit(solution)/shard_map/ppermute | solution.py:20
  15.6 2.2 copy.184
  17.9 1.1 collective-permute-done.1
  20.0 4.7 %collective-permute-start.3 = (f32[224,10,1]{0,1,2:T(8,128)S(1)}, f32[224,10,1]{0,1,2:T(8,128)S(1)}, u32[]{:S(2)}, u32[]{:S(2)}) collective-permute-start(f32[224,10,1]{0,1,2:T(8,128)S(1)} %get-tuple-element.29), channel_id=1, source_target_pairs={{0,1},{1,2},{2,3},{3,4},{4,5},{5,6},{6,7},{8,9},{9,10},{10,11},{11... | collective-permute-start | bytes 26888 | tf_op jit(solution)/shard_map/ppermute | solution.py:20
  24.8 1.9 collective-permute-start.2
  27.6 2.3 collective-permute-done.2
  29.8 2.7 add_reduce_fusion.3
  32.8 6.5 %broadcast_multiply_fusion.7 = (f32[224,9,257]{0,1,2:T(8,128)S(1)}, f32[224,9,257]{0,1,2:T(8,128)S(1)}) fusion(f32[9,257]{0,1:T(8,128)S(1)} %copy.183, f32[224,10,257]{0,1,2:T(8,128)} %copy-done.1, f32[224,10,1]{0,1,2:T(8,128)S(1)} %collective-permute-done.2, f32[224,1,256]{0,1,2:T(1,128)S(1)} %copy.181, f32[224,8,256]{0,1,2:T(8,128)S(1)} %copy.184, ...), kind=kLoop, calls=%fused_computation.35 | loop fusion | flops 3626784 | bytes 10601764 | tf_op jit(solution)/shard_map/mul | solution.py:39
  40.3 1.3 copy-done.11
  42.1 1.3 collective-permute-start.5
  43.6 4.7 %collective-permute-start.4 = (f32[224,1,256]{2,0,1:T(8,128)S(1)}, f32[224,1,256]{2,0,1:T(8,128)S(1)}, u32[]{:S(2)}, u32[]{:S(2)}) collective-permute-start(f32[224,1,256]{2,0,1:T(8,128)S(1)} %copy.187), channel_id=1, source_target_pairs={{0,8},{8,16},{16,24},{1,9},{9,17},{17,25},{2,10},{10,18},{18,26},{... | collective-permute-start | bytes 688136 | tf_op jit(solution)/shard_map/ppermute | solution.py:20
  48.3 2.0 collective-permute-done.5
  50.5 1.7 collective-permute-done.4
  53.3 5.5 %collective-permute-start.7 = (f32[224,10,1]{0,1,2:T(8,128)S(1)}, f32[224,10,1]{0,1,2:T(8,128)S(1)}, u32[]{:S(2)}, u32[]{:S(2)}) collective-permute-start(f32[224,10,1]{0,1,2:T(8,128)S(1)} %get-tuple-element.27), channel_id=1, source_target_pairs={{0,1},{1,2},{2,3},{3,4},{4,5},{5,6},{6,7},{8,9},{9,10},{10,11},{11... | collective-permute-start | bytes 26888 | tf_op jit(solution)/shard_map/ppermute | solution.py:20
  58.8 2.1 collective-permute-start.6
  60.9 2.4 maximum_maximum_fusion.1
  63.9 1.5 copy-done.2
  65.3 2.8 add_reduce_fusion.2
  68.4 8.4 %broadcast_multiply_fusion.5 = (f32[224,9,257]{0,1,2:T(8,128)S(1)}, f32[224,9,257]{0,1,2:T(8,128)}) fusion(f32[9,257]{0,1:T(8,128)S(1)} %copy.192, f32[224,10,257]{0,1,2:T(8,128)} %copy-done.2, f32[224,10,1]{0,1,2:T(8,128)S(1)} %collective-permute-done.6, f32[224,1,256]{0,1,2:T(1,128)S(1)} %copy.190, f32[224,8,256]{0,1,2:T(8,128)} %copy-done.11, ...), kind=kLoop, calls=%fused_computation.33 | loop fusion | flops 3626784 | bytes 10601764 | tf_op jit(solution)/shard_map/mul | solution.py:39
  76.7 3.8 %fusion.12 = f32[224,8,256]{0,1,2:T(8,128)S(1)} fusion(f32[224,8,256]{0,1,2:T(8,128)S(1)} %copy-done.13, f32[224,9,257]{0,1,2:T(8,128)} %get-tuple-element.19, f32[224,9,257]{0,1,2:T(8,128)S(1)} %get-tuple-element.18, f32[224,8,256]{0,1,2:T(8,128)S(1)} %copy.184), kind=kLoop, calls=%fused_computation.51 | loop fusion | flops 3670016 | bytes 12845056 | tf_op jit(solution)/shard_map/add | solution.py:48
  80.6 1.3 copy-done.8
  82.4 1.3 collective-permute-start.9
  83.8 4.7 %collective-permute-start.8 = (f32[224,1,256]{2,0,1:T(8,128)S(1)}, f32[224,1,256]{2,0,1:T(8,128)S(1)}, u32[]{:S(2)}, u32[]{:S(2)}) collective-permute-start(f32[224,1,256]{2,0,1:T(8,128)S(1)} %copy.194), channel_id=1, source_target_pairs={{0,8},{8,16},{16,24},{1,9},{9,17},{17,25},{2,10},{10,18},{18,26},{... | collective-permute-start | bytes 688136 | tf_op jit(solution)/shard_map/ppermute | solution.py:20
  88.6 1.3 collective-permute-done.9
  90.1 1.5 collective-permute-done.8
  92.6 5.2 %collective-permute-start.11 = (f32[224,10,1]{0,1,2:T(8,128)S(1)}, f32[224,10,1]{0,1,2:T(8,128)S(1)}, u32[]{:S(2)}, u32[]{:S(2)}) collective-permute-start(f32[224,10,1]{0,1,2:T(8,128)S(1)} %get-tuple-element.25), channel_id=1, source_target_pairs={{0,1},{1,2},{2,3},{3,4},{4,5},{5,6},{6,7},{8,9},{9,10},{10,11},{11... | collective-permute-start | bytes 26888 | tf_op jit(solution)/shard_map/ppermute | solution.py:20
  97.8 1.9 collective-permute-start.10
  99.7 2.4 maximum_maximum_fusion.2
  102.9 1.3 copy-done.3
  104.1 2.8 add_reduce_fusion.1
  107.2 8.4 %broadcast_multiply_fusion.3 = (f32[224,9,257]{0,1,2:T(8,128)S(1)}, f32[224,9,257]{0,1,2:T(8,128)}) fusion(f32[9,257]{0,1:T(8,128)S(1)} %copy.199, f32[224,10,257]{0,1,2:T(8,128)} %copy-done.3, f32[224,10,1]{0,1,2:T(8,128)S(1)} %collective-permute-done.10, f32[224,1,256]{0,1,2:T(1,128)S(1)} %copy.197, f32[224,8,256]{0,1,2:T(8,128)} %copy-done.8, ...), kind=kLoop, calls=%fused_computation.31 | loop fusion | flops 3626784 | bytes 10601764 | tf_op jit(solution)/shard_map/mul | solution.py:39
  115.5 3.8 %fusion.9 = f32[224,8,256]{0,1,2:T(8,128)S(1)} fusion(f32[224,8,256]{0,1,2:T(8,128)S(1)} %copy-done.10, f32[224,9,257]{0,1,2:T(8,128)} %get-tuple-element.17, f32[224,9,257]{0,1,2:T(8,128)S(1)} %get-tuple-element.16, f32[224,8,256]{0,1,2:T(8,128)S(1)} %copy.184), kind=kLoop, calls=%fused_computation.45 | loop fusion | flops 3670016 | bytes 12845056 | tf_op jit(solution)/shard_map/add | solution.py:48
  119.4 1.3 copy-done.5
  121.2 1.3 collective-permute-start.13
  122.6 5.0 %collective-permute-start.12 = (f32[224,1,256]{2,0,1:T(8,128)S(1)}, f32[224,1,256]{2,0,1:T(8,128)S(1)}, u32[]{:S(2)}, u32[]{:S(2)}) collective-permute-start(f32[224,1,256]{2,0,1:T(8,128)S(1)} %copy.201), channel_id=1, source_target_pairs={{0,8},{8,16},{16,24},{1,9},{9,17},{17,25},{2,10},{10,18},{18,26},{... | collective-permute-start | bytes 688136 | tf_op jit(solution)/shard_map/ppermute | solution.py:20
  127.6 1.1 collective-permute-done.13
  128.9 1.5 collective-permute-done.12
  131.4 5.4 %collective-permute-start.15 = (f32[224,10,1]{0,1,2:T(8,128)S(1)}, f32[224,10,1]{0,1,2:T(8,128)S(1)}, u32[]{:S(2)}, u32[]{:S(2)}) collective-permute-start(f32[224,10,1]{0,1,2:T(8,128)S(1)} %get-tuple-element.23), channel_id=1, source_target_pairs={{0,1},{1,2},{2,3},{3,4},{4,5},{5,6},{6,7},{8,9},{9,10},{10,11},{11... | collective-permute-start | bytes 26888 | tf_op jit(solution)/shard_map/ppermute | solution.py:20
  136.8 1.9 collective-permute-start.14
  138.7 2.4 maximum_maximum_fusion.3
  141.8 1.3 copy-done.4
  143.1 2.8 add_reduce_fusion
  146.1 8.4 %broadcast_multiply_fusion.1 = (f32[224,9,257]{0,1,2:T(8,128)S(1)}, f32[224,9,257]{0,1,2:T(8,128)}) fusion(f32[9,257]{0,1:T(8,128)S(1)} %copy.206, f32[224,10,257]{0,1,2:T(8,128)} %copy-done.4, f32[224,10,1]{0,1,2:T(8,128)S(1)} %collective-permute-done.14, f32[224,1,256]{0,1,2:T(1,128)S(1)} %copy.204, f32[224,8,256]{0,1,2:T(8,128)} %copy-done.5, ...), kind=kLoop, calls=%fused_computation.29 | loop fusion | flops 3626784 | bytes 10601764 | tf_op jit(solution)/shard_map/mul | solution.py:39
  154.5 3.8 %fusion.6 = f32[224,8,256]{0,1,2:T(8,128)S(1)} fusion(f32[224,8,256]{0,1,2:T(8,128)S(1)} %copy-done.7, f32[224,9,257]{0,1,2:T(8,128)} %get-tuple-element.15, f32[224,9,257]{0,1,2:T(8,128)S(1)} %get-tuple-element.14, f32[224,8,256]{0,1,2:T(8,128)S(1)} %copy.184), kind=kLoop, calls=%fused_computation.39 | loop fusion | flops 3670016 | bytes 12845056 | tf_op jit(solution)/shard_map/add | solution.py:48
  158.3 1.3 copy-done.14
  159.7 5.0 %fusion.18 = f32[224,224]{1,0:T(8,128)} fusion(f32[224,8,256]{0,1,2:T(8,128)S(1)} %fusion.6), kind=kOutput, calls=%fused_computation.62 | convolution fusion | flops 1233125376 | bytes 2035712 | tf_op jit(solution)/shard_map/dot_general | solution.py:65
  164.7 2.6 copy.215
  167.3 2.0 copy.218
  169.3 122.3 %all-reduce.2.cloned.1.call-done = f32[224,224]{1,0:T(8,128)} async-done(((f32[224,224]{1,0:T(8,128)}), f32[224,224]{1,0:T(8,128)}) %all-reduce.2.cloned.1.call-update) | async-done | bytes 200720 | tf_op jit(solution)/shard_map/psum | solution.py:72
  291.6 1.2 fusion.43
  293.1 1.5 cholesky.74
  296.0 1.2 custom-call.8
  297.6 1.5 cholesky.85
  300.6 1.2 custom-call.9
  302.0 1.2 fusion.46
  303.5 1.5 cholesky.96
  306.4 1.2 custom-call.10
  308.0 1.5 cholesky.107
  310.9 1.2 custom-call.11
  312.4 2.5 fusion.49
  314.9 1.6 fusion.50
  316.5 2.0 copy.219
  (100 shorter events, 18.6 us)
Async XLA Ops:
  7.2 284.4 %copy-start = (f32[224,16]{0,1:T(8,128)S(1)}, f32[224,16]{0,1:T(8,128)}, u32[]{:S(2)}) copy-start(f32[224,16]{0,1:T(8,128)} %param.6) | copy-start | bytes 43012
  7.2 284.4 %all-reduce.2.cloned.1.call-start = ((), (), s32[]{:S(2)}) async-start(), calls=%async_computation | async-start | bytes 458752 | tf_op jit(solution)/shard_map/psum | solution.py:72
  9.6 9.4 %collective-permute-start.1 = (f32[224,1,256]{2,0,1:T(8,128)S(1)}, f32[224,1,256]{2,0,1:T(8,128)S(1)}, u32[]{:S(2)}, u32[]{:S(2)}) collective-permute-start(f32[224,1,256]{2,0,1:T(8,128)S(1)} %copy.217), channel_id=1, source_target_pairs={{8,0},{16,8},{24,16},{9,1},{17,9},{25,17},{10,2},{18,10},{26,18},{... | collective-permute-start | bytes 688136 | tf_op jit(solution)/shard_map/ppermute | solution.py:22
  10.9 8.9 %collective-permute-start = (f32[224,1,256]{2,0,1:T(8,128)S(1)}, f32[224,1,256]{2,0,1:T(8,128)S(1)}, u32[]{:S(2)}, u32[]{:S(2)}) collective-permute-start(f32[224,1,256]{2,0,1:T(8,128)S(1)} %copy.216), channel_id=1, source_target_pairs={{0,8},{8,16},{16,24},{1,9},{9,17},{17,25},{2,10},{10,18},{18,26},{... | collective-permute-start | bytes 688136 | tf_op jit(solution)/shard_map/ppermute | solution.py:20
  20.0 6.6 %collective-permute-start.3 = (f32[224,10,1]{0,1,2:T(8,128)S(1)}, f32[224,10,1]{0,1,2:T(8,128)S(1)}, u32[]{:S(2)}, u32[]{:S(2)}) collective-permute-start(f32[224,10,1]{0,1,2:T(8,128)S(1)} %get-tuple-element.29), channel_id=1, source_target_pairs={{0,1},{1,2},{2,3},{3,4},{4,5},{5,6},{6,7},{8,9},{9,10},{10,11},{11... | collective-permute-start | bytes 26888 | tf_op jit(solution)/shard_map/ppermute | solution.py:20
  24.8 5.1 %collective-permute-start.2 = (f32[224,10,1]{0,1,2:T(8,128)S(1)}, f32[224,10,1]{0,1,2:T(8,128)S(1)}, u32[]{:S(2)}, u32[]{:S(2)}) collective-permute-start(f32[224,10,1]{0,1,2:T(8,128)S(1)} %get-tuple-element.28), channel_id=1, source_target_pairs={{1,0},{2,1},{3,2},{4,3},{5,4},{6,5},{7,6},{9,8},{10,9},{11,10},{12... | collective-permute-start | bytes 26888 | tf_op jit(solution)/shard_map/ppermute | solution.py:22
  27.5 2.3 copy-start.1
  40.3 1.4 copy-start.11
  42.1 8.2 %collective-permute-start.5 = (f32[224,1,256]{2,0,1:T(8,128)S(1)}, f32[224,1,256]{2,0,1:T(8,128)S(1)}, u32[]{:S(2)}, u32[]{:S(2)}) collective-permute-start(f32[224,1,256]{2,0,1:T(8,128)S(1)} %copy.188), channel_id=1, source_target_pairs={{8,0},{16,8},{24,16},{9,1},{17,9},{25,17},{10,2},{18,10},{26,18},{... | collective-permute-start | bytes 688136 | tf_op jit(solution)/shard_map/ppermute | solution.py:22
  43.6 8.6 %collective-permute-start.4 = (f32[224,1,256]{2,0,1:T(8,128)S(1)}, f32[224,1,256]{2,0,1:T(8,128)S(1)}, u32[]{:S(2)}, u32[]{:S(2)}) collective-permute-start(f32[224,1,256]{2,0,1:T(8,128)S(1)} %copy.187), channel_id=1, source_target_pairs={{0,8},{8,16},{16,24},{1,9},{9,17},{17,25},{2,10},{10,18},{18,26},{... | collective-permute-start | bytes 688136 | tf_op jit(solution)/shard_map/ppermute | solution.py:20
  52.4 13.0 %copy-start.12 = (f32[224,8,256]{0,1,2:T(8,128)S(1)}, f32[224,8,256]{0,1,2:T(8,128)}, u32[]{:S(2)}) copy-start(f32[224,8,256]{0,1,2:T(8,128)} %copy-done.11) | copy-start | bytes 5505028
  53.3 7.7 %collective-permute-start.7 = (f32[224,10,1]{0,1,2:T(8,128)S(1)}, f32[224,10,1]{0,1,2:T(8,128)S(1)}, u32[]{:S(2)}, u32[]{:S(2)}) collective-permute-start(f32[224,10,1]{0,1,2:T(8,128)S(1)} %get-tuple-element.27), channel_id=1, source_target_pairs={{0,1},{1,2},{2,3},{3,4},{4,5},{5,6},{6,7},{8,9},{9,10},{10,11},{11... | collective-permute-start | bytes 26888 | tf_op jit(solution)/shard_map/ppermute | solution.py:20
  58.8 5.1 %collective-permute-start.6 = (f32[224,10,1]{0,1,2:T(8,128)S(1)}, f32[224,10,1]{0,1,2:T(8,128)S(1)}, u32[]{:S(2)}, u32[]{:S(2)}) collective-permute-start(f32[224,10,1]{0,1,2:T(8,128)S(1)} %get-tuple-element.26), channel_id=1, source_target_pairs={{1,0},{2,1},{3,2},{4,3},{5,4},{6,5},{7,6},{9,8},{10,9},{11,10},{12... | collective-permute-start | bytes 26888 | tf_op jit(solution)/shard_map/ppermute | solution.py:22
  63.4 2.0 copy-start.2
  68.3 8.4 %copy-start.13 = (f32[224,8,256]{0,1,2:T(8,128)S(1)}, f32[224,8,256]{0,1,2:T(8,128)}, u32[]{:S(2)}) copy-start(f32[224,8,256]{0,1,2:T(8,128)} %copy-done.11) | copy-start | bytes 5505028
  80.6 1.4 copy-start.8
  82.4 7.5 %collective-permute-start.9 = (f32[224,1,256]{2,0,1:T(8,128)S(1)}, f32[224,1,256]{2,0,1:T(8,128)S(1)}, u32[]{:S(2)}, u32[]{:S(2)}) collective-permute-start(f32[224,1,256]{2,0,1:T(8,128)S(1)} %copy.195), channel_id=1, source_target_pairs={{8,0},{16,8},{24,16},{9,1},{17,9},{25,17},{10,2},{18,10},{26,18},{... | collective-permute-start | bytes 688136 | tf_op jit(solution)/shard_map/ppermute | solution.py:22
  83.8 7.7 %collective-permute-start.8 = (f32[224,1,256]{2,0,1:T(8,128)S(1)}, f32[224,1,256]{2,0,1:T(8,128)S(1)}, u32[]{:S(2)}, u32[]{:S(2)}) collective-permute-start(f32[224,1,256]{2,0,1:T(8,128)S(1)} %copy.194), channel_id=1, source_target_pairs={{0,8},{8,16},{16,24},{1,9},{9,17},{17,25},{2,10},{10,18},{18,26},{... | collective-permute-start | bytes 688136 | tf_op jit(solution)/shard_map/ppermute | solution.py:20
  91.7 12.5 %copy-start.9 = (f32[224,8,256]{0,1,2:T(8,128)S(1)}, f32[224,8,256]{0,1,2:T(8,128)}, u32[]{:S(2)}) copy-start(f32[224,8,256]{0,1,2:T(8,128)} %copy-done.8) | copy-start | bytes 5505028
  92.6 7.2 %collective-permute-start.11 = (f32[224,10,1]{0,1,2:T(8,128)S(1)}, f32[224,10,1]{0,1,2:T(8,128)S(1)}, u32[]{:S(2)}, u32[]{:S(2)}) collective-permute-start(f32[224,10,1]{0,1,2:T(8,128)S(1)} %get-tuple-element.25), channel_id=1, source_target_pairs={{0,1},{1,2},{2,3},{3,4},{4,5},{5,6},{6,7},{8,9},{9,10},{10,11},{11... | collective-permute-start | bytes 26888 | tf_op jit(solution)/shard_map/ppermute | solution.py:20
  97.8 5.1 %collective-permute-start.10 = (f32[224,10,1]{0,1,2:T(8,128)S(1)}, f32[224,10,1]{0,1,2:T(8,128)S(1)}, u32[]{:S(2)}, u32[]{:S(2)}) collective-permute-start(f32[224,10,1]{0,1,2:T(8,128)S(1)} %get-tuple-element.24), channel_id=1, source_target_pairs={{1,0},{2,1},{3,2},{4,3},{5,4},{6,5},{7,6},{9,8},{10,9},{11,10},{12... | collective-permute-start | bytes 26888 | tf_op jit(solution)/shard_map/ppermute | solution.py:22
  102.2 2.0 copy-start.3
  107.1 8.4 %copy-start.10 = (f32[224,8,256]{0,1,2:T(8,128)S(1)}, f32[224,8,256]{0,1,2:T(8,128)}, u32[]{:S(2)}) copy-start(f32[224,8,256]{0,1,2:T(8,128)} %copy-done.8) | copy-start | bytes 5505028
  119.4 1.4 copy-start.5
  121.2 7.5 %collective-permute-start.13 = (f32[224,1,256]{2,0,1:T(8,128)S(1)}, f32[224,1,256]{2,0,1:T(8,128)S(1)}, u32[]{:S(2)}, u32[]{:S(2)}) collective-permute-start(f32[224,1,256]{2,0,1:T(8,128)S(1)} %copy.202), channel_id=1, source_target_pairs={{8,0},{16,8},{24,16},{9,1},{17,9},{25,17},{10,2},{18,10},{26,18},{... | collective-permute-start | bytes 688136 | tf_op jit(solution)/shard_map/ppermute | solution.py:22
  122.6 7.7 %collective-permute-start.12 = (f32[224,1,256]{2,0,1:T(8,128)S(1)}, f32[224,1,256]{2,0,1:T(8,128)S(1)}, u32[]{:S(2)}, u32[]{:S(2)}) collective-permute-start(f32[224,1,256]{2,0,1:T(8,128)S(1)} %copy.201), channel_id=1, source_target_pairs={{0,8},{8,16},{16,24},{1,9},{9,17},{17,25},{2,10},{10,18},{18,26},{... | collective-permute-start | bytes 688136 | tf_op jit(solution)/shard_map/ppermute | solution.py:20
  130.5 12.6 %copy-start.6 = (f32[224,8,256]{0,1,2:T(8,128)S(1)}, f32[224,8,256]{0,1,2:T(8,128)}, u32[]{:S(2)}) copy-start(f32[224,8,256]{0,1,2:T(8,128)} %copy-done.5) | copy-start | bytes 5505028
  131.4 7.3 %collective-permute-start.15 = (f32[224,10,1]{0,1,2:T(8,128)S(1)}, f32[224,10,1]{0,1,2:T(8,128)S(1)}, u32[]{:S(2)}, u32[]{:S(2)}) collective-permute-start(f32[224,10,1]{0,1,2:T(8,128)S(1)} %get-tuple-element.23), channel_id=1, source_target_pairs={{0,1},{1,2},{2,3},{3,4},{4,5},{5,6},{6,7},{8,9},{9,10},{10,11},{11... | collective-permute-start | bytes 26888 | tf_op jit(solution)/shard_map/ppermute | solution.py:20
  136.8 5.1 %collective-permute-start.14 = (f32[224,10,1]{0,1,2:T(8,128)S(1)}, f32[224,10,1]{0,1,2:T(8,128)S(1)}, u32[]{:S(2)}, u32[]{:S(2)}) collective-permute-start(f32[224,10,1]{0,1,2:T(8,128)S(1)} %get-tuple-element.22), channel_id=1, source_target_pairs={{1,0},{2,1},{3,2},{4,3},{5,4},{6,5},{7,6},{9,8},{10,9},{11,10},{12... | collective-permute-start | bytes 26888 | tf_op jit(solution)/shard_map/ppermute | solution.py:22
  141.1 2.0 copy-start.4
  146.1 8.4 %copy-start.7 = (f32[224,8,256]{0,1,2:T(8,128)S(1)}, f32[224,8,256]{0,1,2:T(8,128)}, u32[]{:S(2)}) copy-start(f32[224,8,256]{0,1,2:T(8,128)} %copy-done.5) | copy-start | bytes 5505028
  158.3 1.3 copy-start.14
  167.3 149.2 %copy-start.15 = (f32[224,8,256]{2,1,0:T(8,128)}, f32[224,8,256]{2,1,0:T(8,128)S(1)}, u32[]{:S(2)}) copy-start(f32[224,8,256]{2,1,0:T(8,128)S(1)} %copy.215) | copy-start | bytes 5505028
Sparse Core Ops, SparseCore 0:
  164.8 126.7 all-reduce.1
where the time goes:
time: 326 us; the launch traced here: 325 us
  waiting for transfers between devices  137 us (42%)
  other arithmetic  82.5 us (25%)
  starting transfers between devices  53.1 us (16%)
  local copies, waits for them, and re-layouts  24.8 us (8%)
  between operations  14.7 us (5%)
  matrix products  13 us (4%)
    psum x1, waiting for transfers between devices, shards(): gram_full = lax.psum(local_gram, ('row', 'col'))  122 us
    ppermute x8, starting transfers between devices, padded_2(): lax.ppermute(tail, axis, [(i, (i + 1) % count) for i in range(ends)])  40 us
    mul x4, other arithmetic, smooth_step(): flux_col = weight * diff_col  31.7 us
    unnamed x38, local copies, waits for them, and re-layouts  18.3 us
    ppermute x8, starting transfers between devices, padded_2(): lax.ppermute(head, axis, [((i + 1) % count, i) for i in range(ends)])  13 us
    add x4, other arithmetic, smooth_step(): return centre + tau_step * spread + tau_step * fidelity * (source - centre)  12.4 us
    reduce_sum x4, other arithmetic, smooth_step(): energy_sum = jnp.sum(diff_col * diff_col + diff_row * diff_row, axis=0)  11 us
    ppermute x8, waiting for transfers between devices, padded_2(): lax.ppermute(head, axis, [((i + 1) % count, i) for i in range(ends)])  9.65 us
  transfers between devices with their start and end apart: 17, of which 13 were waited for; matrix products, arithmetic and copies ran while one was open for 5% of the time, Pallas kernels for 0%

commit v1 on v0

--- a/solution.py
+++ b/solution.py
@@ -2,6 +2,7 @@
 import jax.numpy as jnp
 from jax import lax
 from jax.sharding import PartitionSpec as P
+from jax.lax import all_gather
 
 SWEEPS = 4
 SUBIT = 2
@@ -69,7 +70,7 @@
         precision=lax.Precision.HIGHEST,
         preferred_element_type=jnp.float32,
     )
-    gram_full = lax.psum(local_gram, ("row", "col"))
+    gram_full = jnp.sum(all_gather(local_gram, ("row", "col")), 0)
     for turn in range(SUBIT):
         product = jnp.dot(gram_full, basis_now, precision=lax.Precision.HIGHEST)
         basis_now = orthonormal(orthonormal(product))

time: 326 us -> 278 us (0.85)
  waiting for transfers between devices: 137 us -> 87 us
  other arithmetic: 82.5 us -> 86.1 us
    psum x1 -> x0, waiting for transfers between devices: 122 us -> none  [shards(): gram_full = lax.psum(local_gram, ('row', 'col'))]
    all_gather x0 -> x1, waiting for transfers between devices: none -> 72 us  [shards(): gram_full = jnp.sum(all_gather(local_gram, ('row', 'col')), 0)]
    reduce_sum x0 -> x1, other arithmetic: none -> 3.61 us  [shards(): gram_full = jnp.sum(all_gather(local_gram, ('row', 'col')), 0)]
  transfers between devices with their start and end apart: 17 -> 17, of which waited for: 13 -> 13; matrix products, arithmetic and copies ran while one was open for 5% -> 6% of each run, Pallas kernels for 0% -> 0%
where the time goes in v1:
time: 278 us; the launch traced here: 277 us
  waiting for transfers between devices  87 us (31%)
  other arithmetic  86.1 us (31%)
  starting transfers between devices  53.1 us (19%)
  local copies, waits for them, and re-layouts  24.8 us (9%)
  between operations  14.7 us (5%)
  matrix products  11.1 us (4%)
    all_gather x1, waiting for transfers between devices, shards(): gram_full = jnp.sum(all_gather(local_gram, ('row', 'col')), 0)  72 us
    ppermute x8, starting transfers between devices, padded_2(): lax.ppermute(tail, axis, [(i, (i + 1) % count) for i in range(ends)])  40 us
    mul x4, other arithmetic, smooth_step(): flux_col = weight * diff_col  31.7 us
    unnamed x38, local copies, waits for them, and re-layouts  18.3 us
    ppermute x8, starting transfers between devices, padded_2(): lax.ppermute(head, axis, [((i + 1) % count, i) for i in range(ends)])  13 us
    add x4, other arithmetic, smooth_step(): return centre + tau_step * spread + tau_step * fidelity * (source - centre)  12.4 us
    reduce_sum x4, other arithmetic, smooth_step(): energy_sum = jnp.sum(diff_col * diff_col + diff_row * diff_row, axis=0)  11 us
    ppermute x8, waiting for transfers between devices, padded_2(): lax.ppermute(head, axis, [((i + 1) % count, i) for i in range(ends)])  9.65 us
  transfers between devices with their start and end apart: 17, of which 13 were waited for; matrix products, arithmetic and copies ran while one was open for 6% of the time, Pallas kernels for 0%

profile of v1, /device:TPU:1, one launch (start us, length us, event | category | flops | bytes accessed | tf_op | source)
XLA Modules:
  0.0 276.8 jit_solution(650038881157199222)
XLA Ops:
  7.2 2.4 fusion.42
  9.6 1.3 collective-permute-start.1
  10.9 4.7 %collective-permute-start = (f32[224,1,256]{2,0,1:T(8,128)S(1)}, f32[224,1,256]{2,0,1:T(8,128)S(1)}, u32[]{:S(2)}, u32[]{:S(2)}) collective-permute-start(f32[224,1,256]{2,0,1:T(8,128)S(1)} %copy.216), channel_id=1, source_target_pairs={{0,8},{8,16},{16,24},{1,9},{9,17},{17,25},{2,10},{10,18},{18,26},{... | collective-permute-start | bytes 688136 | tf_op jit(solution)/shard_map/ppermute | solution.py:21
  15.6 2.2 copy.184
  17.9 1.1 collective-permute-done.1
  20.0 4.7 %collective-permute-start.3 = (f32[224,10,1]{0,1,2:T(8,128)S(1)}, f32[224,10,1]{0,1,2:T(8,128)S(1)}, u32[]{:S(2)}, u32[]{:S(2)}) collective-permute-start(f32[224,10,1]{0,1,2:T(8,128)S(1)} %get-tuple-element.29), channel_id=1, source_target_pairs={{0,1},{1,2},{2,3},{3,4},{4,5},{5,6},{6,7},{8,9},{9,10},{10,11},{11... | collective-permute-start | bytes 26888 | tf_op jit(solution)/shard_map/ppermute | solution.py:21
  24.8 1.9 collective-permute-start.2
  27.6 2.3 collective-permute-done.2
  29.8 2.7 add_reduce_fusion.3
  32.8 6.5 %broadcast_multiply_fusion.7 = (f32[224,9,257]{0,1,2:T(8,128)S(1)}, f32[224,9,257]{0,1,2:T(8,128)S(1)}) fusion(f32[9,257]{0,1:T(8,128)S(1)} %copy.183, f32[224,10,257]{0,1,2:T(8,128)} %copy-done.1, f32[224,10,1]{0,1,2:T(8,128)S(1)} %collective-permute-done.2, f32[224,1,256]{0,1,2:T(1,128)S(1)} %copy.181, f32[224,8,256]{0,1,2:T(8,128)S(1)} %copy.184, ...), kind=kLoop, calls=%fused_computation.35 | loop fusion | flops 3626784 | bytes 10601764 | tf_op jit(solution)/shard_map/mul | solution.py:40
  39.4 1.0 fusion.15
  40.3 1.3 copy-done.11
  42.1 1.3 collective-permute-start.5
  43.6 4.7 %collective-permute-start.4 = (f32[224,1,256]{2,0,1:T(8,128)S(1)}, f32[224,1,256]{2,0,1:T(8,128)S(1)}, u32[]{:S(2)}, u32[]{:S(2)}) collective-permute-start(f32[224,1,256]{2,0,1:T(8,128)S(1)} %copy.187), channel_id=1, source_target_pairs={{0,8},{8,16},{16,24},{1,9},{9,17},{17,25},{2,10},{10,18},{18,26},{... | collective-permute-start | bytes 688136 | tf_op jit(solution)/shard_map/ppermute | solution.py:21
  48.3 2.0 collective-permute-done.5
  50.5 1.7 collective-permute-done.4
  53.3 5.5 %collective-permute-start.7 = (f32[224,10,1]{0,1,2:T(8,128)S(1)}, f32[224,10,1]{0,1,2:T(8,128)S(1)}, u32[]{:S(2)}, u32[]{:S(2)}) collective-permute-start(f32[224,10,1]{0,1,2:T(8,128)S(1)} %get-tuple-element.27), channel_id=1, source_target_pairs={{0,1},{1,2},{2,3},{3,4},{4,5},{5,6},{6,7},{8,9},{9,10},{10,11},{11... | collective-permute-start | bytes 26888 | tf_op jit(solution)/shard_map/ppermute | solution.py:21
  58.8 2.1 collective-permute-start.6
  60.9 2.4 maximum_maximum_fusion.1
  63.9 1.5 copy-done.2
  65.3 2.8 add_reduce_fusion.2
  68.4 8.4 %broadcast_multiply_fusion.5 = (f32[224,9,257]{0,1,2:T(8,128)S(1)}, f32[224,9,257]{0,1,2:T(8,128)}) fusion(f32[9,257]{0,1:T(8,128)S(1)} %copy.192, f32[224,10,257]{0,1,2:T(8,128)} %copy-done.2, f32[224,10,1]{0,1,2:T(8,128)S(1)} %collective-permute-done.6, f32[224,1,256]{0,1,2:T(1,128)S(1)} %copy.190, f32[224,8,256]{0,1,2:T(8,128)} %copy-done.11, ...), kind=kLoop, calls=%fused_computation.33 | loop fusion | flops 3626784 | bytes 10601764 | tf_op jit(solution)/shard_map/mul | solution.py:40
  76.7 3.8 %fusion.12 = f32[224,8,256]{0,1,2:T(8,128)S(1)} fusion(f32[224,8,256]{0,1,2:T(8,128)S(1)} %copy-done.13, f32[224,9,257]{0,1,2:T(8,128)} %get-tuple-element.19, f32[224,9,257]{0,1,2:T(8,128)S(1)} %get-tuple-element.18, f32[224,8,256]{0,1,2:T(8,128)S(1)} %copy.184), kind=kLoop, calls=%fused_computation.51 | loop fusion | flops 3670016 | bytes 12845056 | tf_op jit(solution)/shard_map/add | solution.py:49
  80.6 1.3 copy-done.8
  82.4 1.3 collective-permute-start.9
  83.8 4.7 %collective-permute-start.8 = (f32[224,1,256]{2,0,1:T(8,128)S(1)}, f32[224,1,256]{2,0,1:T(8,128)S(1)}, u32[]{:S(2)}, u32[]{:S(2)}) collective-permute-start(f32[224,1,256]{2,0,1:T(8,128)S(1)} %copy.194), channel_id=1, source_target_pairs={{0,8},{8,16},{16,24},{1,9},{9,17},{17,25},{2,10},{10,18},{18,26},{... | collective-permute-start | bytes 688136 | tf_op jit(solution)/shard_map/ppermute | solution.py:21
  88.6 1.3 collective-permute-done.9
  90.1 1.5 collective-permute-done.8
  92.6 5.2 %collective-permute-start.11 = (f32[224,10,1]{0,1,2:T(8,128)S(1)}, f32[224,10,1]{0,1,2:T(8,128)S(1)}, u32[]{:S(2)}, u32[]{:S(2)}) collective-permute-start(f32[224,10,1]{0,1,2:T(8,128)S(1)} %get-tuple-element.25), channel_id=1, source_target_pairs={{0,1},{1,2},{2,3},{3,4},{4,5},{5,6},{6,7},{8,9},{9,10},{10,11},{11... | collective-permute-start | bytes 26888 | tf_op jit(solution)/shard_map/ppermute | solution.py:21
  97.8 1.9 collective-permute-start.10
  99.7 2.4 maximum_maximum_fusion.2
  102.9 1.3 copy-done.3
  104.1 2.8 add_reduce_fusion.1
  107.2 8.4 %broadcast_multiply_fusion.3 = (f32[224,9,257]{0,1,2:T(8,128)S(1)}, f32[224,9,257]{0,1,2:T(8,128)}) fusion(f32[9,257]{0,1:T(8,128)S(1)} %copy.199, f32[224,10,257]{0,1,2:T(8,128)} %copy-done.3, f32[224,10,1]{0,1,2:T(8,128)S(1)} %collective-permute-done.10, f32[224,1,256]{0,1,2:T(1,128)S(1)} %copy.197, f32[224,8,256]{0,1,2:T(8,128)} %copy-done.8, ...), kind=kLoop, calls=%fused_computation.31 | loop fusion | flops 3626784 | bytes 10601764 | tf_op jit(solution)/shard_map/mul | solution.py:40
  115.5 3.8 %fusion.9 = f32[224,8,256]{0,1,2:T(8,128)S(1)} fusion(f32[224,8,256]{0,1,2:T(8,128)S(1)} %copy-done.10, f32[224,9,257]{0,1,2:T(8,128)} %get-tuple-element.17, f32[224,9,257]{0,1,2:T(8,128)S(1)} %get-tuple-element.16, f32[224,8,256]{0,1,2:T(8,128)S(1)} %copy.184), kind=kLoop, calls=%fused_computation.45 | loop fusion | flops 3670016 | bytes 12845056 | tf_op jit(solution)/shard_map/add | solution.py:49
  119.4 1.3 copy-done.5
  121.2 1.3 collective-permute-start.13
  122.6 5.0 %collective-permute-start.12 = (f32[224,1,256]{2,0,1:T(8,128)S(1)}, f32[224,1,256]{2,0,1:T(8,128)S(1)}, u32[]{:S(2)}, u32[]{:S(2)}) collective-permute-start(f32[224,1,256]{2,0,1:T(8,128)S(1)} %copy.201), channel_id=1, source_target_pairs={{0,8},{8,16},{16,24},{1,9},{9,17},{17,25},{2,10},{10,18},{18,26},{... | collective-permute-start | bytes 688136 | tf_op jit(solution)/shard_map/ppermute | solution.py:21
  127.6 1.1 collective-permute-done.13
  128.9 1.5 collective-permute-done.12
  131.4 5.4 %collective-permute-start.15 = (f32[224,10,1]{0,1,2:T(8,128)S(1)}, f32[224,10,1]{0,1,2:T(8,128)S(1)}, u32[]{:S(2)}, u32[]{:S(2)}) collective-permute-start(f32[224,10,1]{0,1,2:T(8,128)S(1)} %get-tuple-element.23), channel_id=1, source_target_pairs={{0,1},{1,2},{2,3},{3,4},{4,5},{5,6},{6,7},{8,9},{9,10},{10,11},{11... | collective-permute-start | bytes 26888 | tf_op jit(solution)/shard_map/ppermute | solution.py:21
  136.8 1.9 collective-permute-start.14
  138.7 2.4 maximum_maximum_fusion.3
  141.8 1.3 copy-done.4
  143.1 2.8 add_reduce_fusion
  146.1 8.4 %broadcast_multiply_fusion.1 = (f32[224,9,257]{0,1,2:T(8,128)S(1)}, f32[224,9,257]{0,1,2:T(8,128)}) fusion(f32[9,257]{0,1:T(8,128)S(1)} %copy.206, f32[224,10,257]{0,1,2:T(8,128)} %copy-done.4, f32[224,10,1]{0,1,2:T(8,128)S(1)} %collective-permute-done.14, f32[224,1,256]{0,1,2:T(1,128)S(1)} %copy.204, f32[224,8,256]{0,1,2:T(8,128)} %copy-done.5, ...), kind=kLoop, calls=%fused_computation.29 | loop fusion | flops 3626784 | bytes 10601764 | tf_op jit(solution)/shard_map/mul | solution.py:40
  154.5 3.8 %fusion.6 = f32[224,8,256]{0,1,2:T(8,128)S(1)} fusion(f32[224,8,256]{0,1,2:T(8,128)S(1)} %copy-done.7, f32[224,9,257]{0,1,2:T(8,128)} %get-tuple-element.15, f32[224,9,257]{0,1,2:T(8,128)S(1)} %get-tuple-element.14, f32[224,8,256]{0,1,2:T(8,128)S(1)} %copy.184), kind=kLoop, calls=%fused_computation.39 | loop fusion | flops 3670016 | bytes 12845056 | tf_op jit(solution)/shard_map/add | solution.py:49
  158.3 1.4 copy-done.14
  159.7 5.0 %fusion.18 = f32[224,224]{1,0:T(8,128)} fusion(f32[224,8,256]{0,1,2:T(8,128)S(1)} %fusion.6), kind=kOutput, calls=%fused_computation.62 | convolution fusion | flops 1233125376 | bytes 2035712 | tf_op jit(solution)/shard_map/dot_general | solution.py:66
  164.8 2.6 copy.215
  167.4 2.0 copy.218
  169.3 72.0 %all-gather.3.cloned.1.call-done = f32[7168,224]{1,0:T(8,128)} async-done(((f32[224,224]{1,0:T(8,128)}), f32[7168,224]{1,0:T(8,128)}) %all-gather.3.cloned.1.call-update) | async-done | bytes 6422544 | tf_op jit(solution)/shard_map/all_gather | solution.py:73
  241.4 3.6 %reduce_sum.49 = f32[224,224]{1,0:T(8,128)S(1)} reduce(f32[32,224,224]{2,1,0:T(8,128)} %bitcast.74, f32[]{:T(128)} %constant.38.clone.1), dimensions={0}, to_apply=%region_4.0 | reduce | flops 1555456 | bytes 6623236 | tf_op jit(solution)/shard_map/reduce_sum | solution.py:73
  245.5 1.5 cholesky.74
  248.4 1.2 custom-call.8
  250.1 1.5 cholesky.85
  253.0 1.2 custom-call.9
  255.0 1.5 cholesky.96
  257.9 1.2 custom-call.10
  259.5 1.5 cholesky.107
  262.4 1.2 custom-call.11
  263.9 2.5 fusion.49
  266.4 1.6 fusion.50
  268.0 2.0 copy.219
  (101 shorter events, 18.2 us)
Async XLA Ops:
  7.2 237.8 %copy-start = (f32[224,16]{0,1:T(8,128)S(1)}, f32[224,16]{0,1:T(8,128)}, u32[]{:S(2)}) copy-start(f32[224,16]{0,1:T(8,128)} %param.6) | copy-start | bytes 43012
  7.2 234.2 %all-gather.3.cloned.1.call-start = ((), (), s32[]{:S(2)}) async-start(), calls=%async_computation | async-start | bytes 7569408 | tf_op jit(solution)/shard_map/all_gather | solution.py:73
  9.6 9.4 %collective-permute-start.1 = (f32[224,1,256]{2,0,1:T(8,128)S(1)}, f32[224,1,256]{2,0,1:T(8,128)S(1)}, u32[]{:S(2)}, u32[]{:S(2)}) collective-permute-start(f32[224,1,256]{2,0,1:T(8,128)S(1)} %copy.217), channel_id=1, source_target_pairs={{8,0},{16,8},{24,16},{9,1},{17,9},{25,17},{10,2},{18,10},{26,18},{... | collective-permute-start | bytes 688136 | tf_op jit(solution)/shard_map/ppermute | solution.py:23
  10.9 8.9 %collective-permute-start = (f32[224,1,256]{2,0,1:T(8,128)S(1)}, f32[224,1,256]{2,0,1:T(8,128)S(1)}, u32[]{:S(2)}, u32[]{:S(2)}) collective-permute-start(f32[224,1,256]{2,0,1:T(8,128)S(1)} %copy.216), channel_id=1, source_target_pairs={{0,8},{8,16},{16,24},{1,9},{9,17},{17,25},{2,10},{10,18},{18,26},{... | collective-permute-start | bytes 688136 | tf_op jit(solution)/shard_map/ppermute | solution.py:21
  20.0 6.6 %collective-permute-start.3 = (f32[224,10,1]{0,1,2:T(8,128)S(1)}, f32[224,10,1]{0,1,2:T(8,128)S(1)}, u32[]{:S(2)}, u32[]{:S(2)}) collective-permute-start(f32[224,10,1]{0,1,2:T(8,128)S(1)} %get-tuple-element.29), channel_id=1, source_target_pairs={{0,1},{1,2},{2,3},{3,4},{4,5},{5,6},{6,7},{8,9},{9,10},{10,11},{11... | collective-permute-start | bytes 26888 | tf_op jit(solution)/shard_map/ppermute | solution.py:21
  24.8 5.1 %collective-permute-start.2 = (f32[224,10,1]{0,1,2:T(8,128)S(1)}, f32[224,10,1]{0,1,2:T(8,128)S(1)}, u32[]{:S(2)}, u32[]{:S(2)}) collective-permute-start(f32[224,10,1]{0,1,2:T(8,128)S(1)} %get-tuple-element.28), channel_id=1, source_target_pairs={{1,0},{2,1},{3,2},{4,3},{5,4},{6,5},{7,6},{9,8},{10,9},{11,10},{12... | collective-permute-start | bytes 26888 | tf_op jit(solution)/shard_map/ppermute | solution.py:23
  27.5 2.3 copy-start.1
  40.3 1.4 copy-start.11
  42.1 8.2 %collective-permute-start.5 = (f32[224,1,256]{2,0,1:T(8,128)S(1)}, f32[224,1,256]{2,0,1:T(8,128)S(1)}, u32[]{:S(2)}, u32[]{:S(2)}) collective-permute-start(f32[224,1,256]{2,0,1:T(8,128)S(1)} %copy.188), channel_id=1, source_target_pairs={{8,0},{16,8},{24,16},{9,1},{17,9},{25,17},{10,2},{18,10},{26,18},{... | collective-permute-start | bytes 688136 | tf_op jit(solution)/shard_map/ppermute | solution.py:23
  43.6 8.6 %collective-permute-start.4 = (f32[224,1,256]{2,0,1:T(8,128)S(1)}, f32[224,1,256]{2,0,1:T(8,128)S(1)}, u32[]{:S(2)}, u32[]{:S(2)}) collective-permute-start(f32[224,1,256]{2,0,1:T(8,128)S(1)} %copy.187), channel_id=1, source_target_pairs={{0,8},{8,16},{16,24},{1,9},{9,17},{17,25},{2,10},{10,18},{18,26},{... | collective-permute-start | bytes 688136 | tf_op jit(solution)/shard_map/ppermute | solution.py:21
  52.4 13.0 %copy-start.12 = (f32[224,8,256]{0,1,2:T(8,128)S(1)}, f32[224,8,256]{0,1,2:T(8,128)}, u32[]{:S(2)}) copy-start(f32[224,8,256]{0,1,2:T(8,128)} %copy-done.11) | copy-start | bytes 5505028
  53.3 7.7 %collective-permute-start.7 = (f32[224,10,1]{0,1,2:T(8,128)S(1)}, f32[224,10,1]{0,1,2:T(8,128)S(1)}, u32[]{:S(2)}, u32[]{:S(2)}) collective-permute-start(f32[224,10,1]{0,1,2:T(8,128)S(1)} %get-tuple-element.27), channel_id=1, source_target_pairs={{0,1},{1,2},{2,3},{3,4},{4,5},{5,6},{6,7},{8,9},{9,10},{10,11},{11... | collective-permute-start | bytes 26888 | tf_op jit(solution)/shard_map/ppermute | solution.py:21
  58.8 5.1 %collective-permute-start.6 = (f32[224,10,1]{0,1,2:T(8,128)S(1)}, f32[224,10,1]{0,1,2:T(8,128)S(1)}, u32[]{:S(2)}, u32[]{:S(2)}) collective-permute-start(f32[224,10,1]{0,1,2:T(8,128)S(1)} %get-tuple-element.26), channel_id=1, source_target_pairs={{1,0},{2,1},{3,2},{4,3},{5,4},{6,5},{7,6},{9,8},{10,9},{11,10},{12... | collective-permute-start | bytes 26888 | tf_op jit(solution)/shard_map/ppermute | solution.py:23
  63.4 2.0 copy-start.2
  68.3 8.4 %copy-start.13 = (f32[224,8,256]{0,1,2:T(8,128)S(1)}, f32[224,8,256]{0,1,2:T(8,128)}, u32[]{:S(2)}) copy-start(f32[224,8,256]{0,1,2:T(8,128)} %copy-done.11) | copy-start | bytes 5505028
  80.6 1.4 copy-start.8
  82.4 7.5 %collective-permute-start.9 = (f32[224,1,256]{2,0,1:T(8,128)S(1)}, f32[224,1,256]{2,0,1:T(8,128)S(1)}, u32[]{:S(2)}, u32[]{:S(2)}) collective-permute-start(f32[224,1,256]{2,0,1:T(8,128)S(1)} %copy.195), channel_id=1, source_target_pairs={{8,0},{16,8},{24,16},{9,1},{17,9},{25,17},{10,2},{18,10},{26,18},{... | collective-permute-start | bytes 688136 | tf_op jit(solution)/shard_map/ppermute | solution.py:23
  83.8 7.7 %collective-permute-start.8 = (f32[224,1,256]{2,0,1:T(8,128)S(1)}, f32[224,1,256]{2,0,1:T(8,128)S(1)}, u32[]{:S(2)}, u32[]{:S(2)}) collective-permute-start(f32[224,1,256]{2,0,1:T(8,128)S(1)} %copy.194), channel_id=1, source_target_pairs={{0,8},{8,16},{16,24},{1,9},{9,17},{17,25},{2,10},{10,18},{18,26},{... | collective-permute-start | bytes 688136 | tf_op jit(solution)/shard_map/ppermute | solution.py:21
  91.7 12.5 %copy-start.9 = (f32[224,8,256]{0,1,2:T(8,128)S(1)}, f32[224,8,256]{0,1,2:T(8,128)}, u32[]{:S(2)}) copy-start(f32[224,8,256]{0,1,2:T(8,128)} %copy-done.8) | copy-start | bytes 5505028
  92.6 7.2 %collective-permute-start.11 = (f32[224,10,1]{0,1,2:T(8,128)S(1)}, f32[224,10,1]{0,1,2:T(8,128)S(1)}, u32[]{:S(2)}, u32[]{:S(2)}) collective-permute-start(f32[224,10,1]{0,1,2:T(8,128)S(1)} %get-tuple-element.25), channel_id=1, source_target_pairs={{0,1},{1,2},{2,3},{3,4},{4,5},{5,6},{6,7},{8,9},{9,10},{10,11},{11... | collective-permute-start | bytes 26888 | tf_op jit(solution)/shard_map/ppermute | solution.py:21
  97.8 5.1 %collective-permute-start.10 = (f32[224,10,1]{0,1,2:T(8,128)S(1)}, f32[224,10,1]{0,1,2:T(8,128)S(1)}, u32[]{:S(2)}, u32[]{:S(2)}) collective-permute-start(f32[224,10,1]{0,1,2:T(8,128)S(1)} %get-tuple-element.24), channel_id=1, source_target_pairs={{1,0},{2,1},{3,2},{4,3},{5,4},{6,5},{7,6},{9,8},{10,9},{11,10},{12... | collective-permute-start | bytes 26888 | tf_op jit(solution)/shard_map/ppermute | solution.py:23
  102.2 2.0 copy-start.3
  107.1 8.4 %copy-start.10 = (f32[224,8,256]{0,1,2:T(8,128)S(1)}, f32[224,8,256]{0,1,2:T(8,128)}, u32[]{:S(2)}) copy-start(f32[224,8,256]{0,1,2:T(8,128)} %copy-done.8) | copy-start | bytes 5505028
  119.4 1.4 copy-start.5
  121.2 7.5 %collective-permute-start.13 = (f32[224,1,256]{2,0,1:T(8,128)S(1)}, f32[224,1,256]{2,0,1:T(8,128)S(1)}, u32[]{:S(2)}, u32[]{:S(2)}) collective-permute-start(f32[224,1,256]{2,0,1:T(8,128)S(1)} %copy.202), channel_id=1, source_target_pairs={{8,0},{16,8},{24,16},{9,1},{17,9},{25,17},{10,2},{18,10},{26,18},{... | collective-permute-start | bytes 688136 | tf_op jit(solution)/shard_map/ppermute | solution.py:23
  122.6 7.7 %collective-permute-start.12 = (f32[224,1,256]{2,0,1:T(8,128)S(1)}, f32[224,1,256]{2,0,1:T(8,128)S(1)}, u32[]{:S(2)}, u32[]{:S(2)}) collective-permute-start(f32[224,1,256]{2,0,1:T(8,128)S(1)} %copy.201), channel_id=1, source_target_pairs={{0,8},{8,16},{16,24},{1,9},{9,17},{17,25},{2,10},{10,18},{18,26},{... | collective-permute-start | bytes 688136 | tf_op jit(solution)/shard_map/ppermute | solution.py:21
  130.5 12.6 %copy-start.6 = (f32[224,8,256]{0,1,2:T(8,128)S(1)}, f32[224,8,256]{0,1,2:T(8,128)}, u32[]{:S(2)}) copy-start(f32[224,8,256]{0,1,2:T(8,128)} %copy-done.5) | copy-start | bytes 5505028
  131.4 7.3 %collective-permute-start.15 = (f32[224,10,1]{0,1,2:T(8,128)S(1)}, f32[224,10,1]{0,1,2:T(8,128)S(1)}, u32[]{:S(2)}, u32[]{:S(2)}) collective-permute-start(f32[224,10,1]{0,1,2:T(8,128)S(1)} %get-tuple-element.23), channel_id=1, source_target_pairs={{0,1},{1,2},{2,3},{3,4},{4,5},{5,6},{6,7},{8,9},{9,10},{10,11},{11... | collective-permute-start | bytes 26888 | tf_op jit(solution)/shard_map/ppermute | solution.py:21
  136.8 5.1 %collective-permute-start.14 = (f32[224,10,1]{0,1,2:T(8,128)S(1)}, f32[224,10,1]{0,1,2:T(8,128)S(1)}, u32[]{:S(2)}, u32[]{:S(2)}) collective-permute-start(f32[224,10,1]{0,1,2:T(8,128)S(1)} %get-tuple-element.22), channel_id=1, source_target_pairs={{1,0},{2,1},{3,2},{4,3},{5,4},{6,5},{7,6},{9,8},{10,9},{11,10},{12... | collective-permute-start | bytes 26888 | tf_op jit(solution)/shard_map/ppermute | solution.py:23
  141.1 2.0 copy-start.4
  146.1 8.4 %copy-start.7 = (f32[224,8,256]{0,1,2:T(8,128)S(1)}, f32[224,8,256]{0,1,2:T(8,128)}, u32[]{:S(2)}) copy-start(f32[224,8,256]{0,1,2:T(8,128)} %copy-done.5) | copy-start | bytes 5505028
  158.3 1.4 copy-start.14
  167.4 77.6 %copy-start.15 = (f32[224,8,256]{2,1,0:T(8,128)}, f32[224,8,256]{2,1,0:T(8,128)S(1)}, u32[]{:S(2)}) copy-start(f32[224,8,256]{2,1,0:T(8,128)S(1)} %copy.215) | copy-start | bytes 5505028
Sparse Core Ops, SparseCore 0:
  164.9 76.4 all-gather.2
